TPU v7x, 256 devices: a whole 4x4x8 slice. The times are simulated.
256 devices in a mesh: scen: 64 (over y, x, z_hi, core), trade: 4 (over z_lo).
Axes of the slice: x: 4, y: 4, z: 8 (z_hi: 2, z_lo: 4; z = z_hi * 4 + z_lo), core: 2. Of those that a mesh axis runs over, the one named last changes fastest.
Arguments:
- payoffs: float32 [12, 12, 12, 4, 8192], P(None, None, None, 'trade', 'scen'), may hold values from -4 to 4
- sweep_counts: int32 [4, 8192], P('trade', 'scen'), may hold values from 1 to 6
- netting_map: int32 [4, 8192], P('trade'), may hold values from 0 to 511
- type_lengths: int32 [8], replicated, may hold values from 1 to 8192, 32768 in all
- type_diffusion: float32 [8], replicated, may hold values from 0.02 to 0.15
- type_discount: float32 [8], replicated, may hold values from 0.01 to 0.12
- factors: float32 [3, 8192], P(None, 'scen'), may hold values from -1 to 1
Outputs:
- exposures: float32 [8192, 512], P('scen', 'trade')
- allocation: float32 [4, 8192], P('trade', 'scen')
All inputs are finite; a program needn't handle non-finite values.
Results may differ from a plain program's by a relative error of at most 0.0055.
Values may be sent and summed in bfloat16 or wider, within the bound.
No kernel may reach another device: no remote copies, remote signals or barrier semaphores. Data moves between devices by JAX's collectives and lax.ppermute only.
A program may use at most 128 MiB of HBM per device.

v0:
```python
import jax
import jax.numpy as jnp
from jax import lax
from jax.sharding import PartitionSpec as P

GRID = 12
NETS = 512
TYPES = 8
MAX_SWEEPS = 6


def cheb_matrix():
    intervals = GRID - 1
    order_index = jnp.arange(GRID, dtype=jnp.float32)
    end_weights = jnp.where((order_index == 0) | (order_index == intervals), 0.5, 1.0).astype(
        jnp.float32
    )
    angles = jnp.pi * order_index[:, None] * order_index[None, :] / intervals
    return 2.0 / intervals * end_weights[:, None] * end_weights[None, :] * jnp.cos(angles)


def cheb_basis(factors):
    factor_basis = []
    for column in range(3):
        point = factors[column]
        recurrence = [jnp.ones_like(point), point]
        for degree in range(2, GRID):
            recurrence.append(2.0 * point * recurrence[-1] - recurrence[-2])
        factor_basis.append(jnp.stack(recurrence[:GRID], 0))
    product = factor_basis[0][:, None, None, :] * factor_basis[1][None, :, None, :]
    product = product * factor_basis[2][None, None, :, :]
    return product.reshape(GRID * GRID * GRID, -1).astype(jnp.bfloat16)


def price(grid_values, counts, trade_index, type_lengths, type_diffusion, type_discount):
    type_ends = jnp.cumsum(type_lengths)
    type_ids = jnp.sum((trade_index[:, None] >= type_ends[None, :]).astype(jnp.int32), axis=1)
    type_hot = (type_ids[:, None] == jnp.arange(TYPES, dtype=jnp.int32)[None, :]).astype(
        jnp.float32
    )
    diffusion = jnp.sum(type_hot * type_diffusion[None, :], axis=1)
    discount = jnp.sum(type_hot * type_discount[None, :], axis=1)

    def smooth_step(degree, field):
        padded = jnp.pad(field, ((1, 1), (1, 1), (1, 1), (0, 0)))
        beside = padded[2:, 1:-1, 1:-1] + padded[:-2, 1:-1, 1:-1]
        beside = beside + padded[1:-1, 2:, 1:-1] + padded[1:-1, :-2, 1:-1]
        beside = beside + padded[1:-1, 1:-1, 2:] + padded[1:-1, 1:-1, :-2]
        updated = field + diffusion * (beside - 6.0 * field) - discount * field
        return jnp.where(degree < counts, updated, field)

    field = lax.fori_loop(0, MAX_SWEEPS, smooth_step, grid_values)
    matrix = cheb_matrix()
    field = jnp.einsum("ai,ijlp->ajlp", matrix, field, precision=lax.Precision.HIGHEST)
    field = jnp.einsum("bj,ajlp->ablp", matrix, field, precision=lax.Precision.HIGHEST)
    field = jnp.einsum("cl,ablp->abcp", matrix, field, precision=lax.Precision.HIGHEST)
    return field.reshape(GRID * GRID * GRID, -1).astype(jnp.bfloat16)


def shards(
    payoffs, sweep_counts, netting_map, type_lengths, type_diffusion, type_discount, factors
):
    trades_here = payoffs.shape[4]
    scen_index = lax.axis_index("scen")
    group_index = lax.axis_index("trade")
    block_size = trades_here * lax.axis_size("scen")
    first_trade = group_index * block_size + scen_index * trades_here
    trade_index = first_trade + jnp.arange(trades_here, dtype=jnp.int32)
    coef_local = price(
        payoffs[:, :, :, 0, :],
        sweep_counts[0],
        trade_index,
        type_lengths,
        type_diffusion,
        type_discount,
    )
    own_sets = lax.dynamic_slice_in_dim(netting_map[0], scen_index * trades_here, trades_here)
    coef_rows = lax.all_gather(coef_local, "trade", axis=1, tiled=True)
    set_ids = lax.all_gather(own_sets, "trade", axis=0, tiled=True)
    sets_here = NETS // lax.axis_size("trade")
    classes = group_index * sets_here + jnp.arange(sets_here, dtype=jnp.int32)
    set_hot = (set_ids[:, None] == classes[None, :]).astype(jnp.bfloat16)
    set_part = jnp.dot(coef_rows, set_hot, preferred_element_type=jnp.float32)
    set_coef = lax.psum(set_part, "scen")
    basis_rows = cheb_basis(factors).astype(jnp.float32)
    totals = lax.dot_general(
        basis_rows, set_coef, (((0,), (0,)), ((), ())), precision=lax.Precision.HIGHEST
    )
    exposures = jnp.maximum(totals, 0.0)
    scen_total = factors.shape[1] * lax.axis_size("scen")
    weight_part = jnp.dot(basis_rows, exposures, precision=lax.Precision.HIGHEST)
    weights = lax.psum(weight_part, "scen") / scen_total
    trade_weights = lax.dot_general(
        coef_rows.astype(jnp.float32),
        weights,
        (((0,), (0,)), ((), ())),
        precision=lax.Precision.HIGHEST,
    )
    alloc_terms = jnp.sum(trade_weights * set_hot.astype(jnp.float32), axis=1)
    allocation = lax.psum_scatter(alloc_terms, "trade", scatter_dimension=0, tiled=True)
    return (exposures, allocation.reshape(1, trades_here))


def solution(mesh):
    return jax.shard_map(
        shards,
        mesh=mesh,
        in_specs=(
            P(None, None, None, "trade", "scen"),
            P("trade", "scen"),
            P("trade", None),
            P(),
            P(),
            P(),
            P(None, "scen"),
        ),
        out_specs=(P("scen", "trade"), P("trade", "scen")),
        check_vma=False,
    )
```

profile of v0, /device:TPU:0, one launch (start us, length us, event | category | flops | bytes accessed | tf_op | source)
XLA Modules:
  0.0 1643.2 jit_solution(8168996887689070114)
XLA Ops:
  7.2 0.0 copy-start
  7.2 0.0 copy-start.5
  7.2 0.0 copy-start.4
  7.2 0.0 copy-start.6
  7.2 0.0 all-gather.3.cloned.1.call-start
  7.3 0.8 reduce-window.8
  8.1 1.3 copy.21
  9.4 0.1 convert_reduce_fusion
  9.5 0.0 copy-done.5
  9.5 0.0 copy-done.4
  9.5 0.1 select_reduce_fusion
  9.6 0.0 copy-done.6
  9.6 5.0 while.15
  9.6 0.1 copy.31
  9.8 0.7 fusion.49
  10.5 0.1 copy.31
  10.6 0.7 fusion.49
  11.3 0.1 copy.31
  11.4 0.7 fusion.49
  12.1 0.1 copy.31
  12.3 0.7 fusion.49
  13.0 0.1 copy.31
  13.1 0.7 fusion.49
  13.8 0.1 copy.31
  13.9 0.7 fusion.49
  14.6 1.6 fusion.13
  16.2 1.7 convolution_bitcast_fusion
  18.0 1.5 fusion.10
  19.5 0.0 copy-start.3
  19.5 0.9 convert_element_type.40
  20.4 0.0 all-gather.3.cloned.1.call-update
  20.4 0.0 all-reduce.5.cloned.1.call-start
  20.4 0.0 copy-done
  20.5 10.5 all-gather
  30.9 0.0 copy-done.3
  31.0 37.2 %all-gather.3.cloned.1.call-done = bf16[1728,512]{1,0:T(8,128)(2,1)} async-done(((bf16[1728,128]{1,0:T(8,128)(2,1)}), bf16[1728,512]{1,0:T(8,128)(2,1)}) %all-gather.3.cloned.1.call-update) | async-done | bytes 1769488 | tf_op jit(solution)/shard_map/all_gather | solution.py:78
  68.2 3.1 fusion.18
  71.3 0.0 all-reduce.5.cloned.1.call-update
  71.3 0.0 all-reduce.7.cloned.1.call-start
  71.4 0.1 stack.6
  71.6 0.1 multiply_convert_fusion
  71.7 0.1 convert_element_type.36
  71.8 773.6 %all-reduce.5.cloned.1.call-done = f32[1728,128]{1,0:T(8,128)} async-done(((f32[1728,128]{1,0:T(8,128)}), f32[1728,128]{1,0:T(8,128)}) %all-reduce.5.cloned.1.call-update) | async-done | bytes 884752 | tf_op jit(solution)/shard_map/psum | solution.py:84
  845.4 1.8 convolution_maximum_fusion
  847.3 0.0 copy-start.2
  847.3 0.0 copy-start.7
  847.3 0.0 copy-start.1
  847.3 1.4 fusion.41
  848.8 0.0 all-reduce.7.cloned.1.call-update
  848.8 0.0 copy-done.7
  848.8 0.6 dynamic-slice.1
  850.0 772.2 %all-reduce.7.cloned.1.call-done = f32[1728,128]{1,0:T(8,128)} async-done(((f32[1728,128]{1,0:T(8,128)}), f32[1728,128]{1,0:T(8,128)}) %all-reduce.7.cloned.1.call-update) | async-done | bytes 884752 | tf_op jit(solution)/shard_map/psum | solution.py:92
  1622.2 0.0 copy-done.1
  1622.2 2.2 fusion.15
  1624.5 0.0 copy-done.2
  1624.5 11.6 all-reduce.1
  1636.0 0.6 dynamic-slice_bitcast_fusion
  (18 shorter events, 0.2 us)
Async XLA Ops:
  7.2 13.3 copy-start
  7.2 2.3 copy-start.5
  7.2 2.3 copy-start.4
  7.2 2.4 copy-start.6
  7.2 61.0 %all-gather.3.cloned.1.call-start = ((), (), s32[]{:S(2)}) async-start(), calls=%async_computation | async-start | bytes 2211840 | tf_op jit(solution)/shard_map/all_gather | solution.py:78
  19.5 11.5 copy-start.3
  20.4 825.0 %all-reduce.5.cloned.1.call-start = ((), (), s32[]{:S(2)}) async-start(), calls=%async_computation.1 | async-start | bytes 1769472 | tf_op jit(solution)/shard_map/psum | solution.py:84
  71.3 1550.9 %all-reduce.7.cloned.1.call-start = ((), (), s32[]{:S(2)}) async-start(), calls=%async_computation.2 | async-start | bytes 1769472 | tf_op jit(solution)/shard_map/psum | solution.py:92
  847.3 777.2 %copy-start.2 = (f32[128,128]{1,0:T(8,128)}, f32[128,128]{1,0:T(8,128)S(1)}, u32[]{:S(2)}) copy-start(f32[128,128]{1,0:T(8,128)S(1)} %convolution_maximum_fusion) | copy-start | bytes 196612
  847.3 1.5 copy-start.7
  847.3 774.9 %copy-start.1 = (bf16[1728,512]{1,0:T(8,128)(2,1)S(1)}, bf16[1728,512]{1,0:T(8,128)(2,1)}, u32[]{:S(2)}) copy-start(bf16[1728,512]{1,0:T(8,128)(2,1)} %all-gather.3.cloned.1.call-done) | copy-start | bytes 5308420
Sparse Core Ops, SparseCore 0:
  20.5 47.6 all-gather.2
  71.4 773.9 all-reduce.4
  848.9 773.2 all-reduce.6
where the time goes:
time: 1640 us
  waiting for transfers between devices  1580 us (96%)
  blocking collectives  22.1 us (1%)
    psum x1, waiting for transfers between devices, shards(): set_coef = lax.psum(set_part, 'scen')  774 us
    psum x1, waiting for transfers between devices, shards(): weights = lax.psum(weight_part, 'scen') / scen_total  772 us
    all_gather x1, waiting for transfers between devices, shards(): coef_rows = lax.all_gather(coef_local, 'trade', axis=1, tiled=True)  37.2 us
  transfers between devices with their start and end apart: 3, of which 3 were waited for; matrix products, arithmetic and copies ran while one was open for 0% of the time, Pallas kernels for 0%

commit v1 on v0

--- a/solution.py
+++ b/solution.py
@@ -7,6 +7,10 @@
 NETS = 512
 TYPES = 8
 MAX_SWEEPS = 6
+
+
+def slot_state(array_here):
+    return jnp.sum(lax.all_gather(array_here, axis_name="scen"), axis=0)
 
 
 def cheb_matrix():
@@ -89,7 +93,7 @@
     exposures = jnp.maximum(totals, 0.0)
     scen_total = factors.shape[1] * lax.axis_size("scen")
     weight_part = jnp.dot(basis_rows, exposures, precision=lax.Precision.HIGHEST)
-    weights = lax.psum(weight_part, "scen") / scen_total
+    weights = slot_state(weight_part) / scen_total
     trade_weights = lax.dot_general(
         coef_rows.astype(jnp.float32),
         weights,

time: 1640 us -> 1260 us (0.77)
  waiting for transfers between devices: 1580 us -> 1180 us
  other arithmetic: 5.28 us -> 23.1 us
    psum x1 -> x0, waiting for transfers between devices: 772 us -> none  [shards(): weights = lax.psum(weight_part, 'scen') / scen_total]
    all_gather x0 -> x1, waiting for transfers between devices: none -> 371 us  [slot_state(): return jnp.sum(lax.all_gather(array_here, axis_name='scen'), axis=0)]
    reduce_sum x0 -> x1, other arithmetic: none -> 17.9 us  [slot_state(): return jnp.sum(lax.all_gather(array_here, axis_name='scen'), axis=0)]
where the time goes in v1:
time: 1260 us
  waiting for transfers between devices  1180 us (94%)
  other arithmetic  23.1 us (2%)
  blocking collectives  18.8 us (1%)
  between operations  14.6 us (1%)
    psum x1, waiting for transfers between devices, shards(): set_coef = lax.psum(set_part, 'scen')  774 us
    all_gather x1, waiting for transfers between devices, slot_state(): return jnp.sum(lax.all_gather(array_here, axis_name='scen'), axis=0)  371 us
    all_gather x1, waiting for transfers between devices, shards(): coef_rows = lax.all_gather(coef_local, 'trade', axis=1, tiled=True)  37.2 us
  transfers between devices with their start and end apart: 3, of which 3 were waited for; matrix products, arithmetic and copies ran while one was open for 0% of the time, Pallas kernels for 0%

profile of v1, /device:TPU:0, one launch (start us, length us, event | category | flops | bytes accessed | tf_op | source)
XLA Modules:
  0.0 1255.5 jit_solution(9175407273311447975)
XLA Ops:
  7.2 0.0 copy-start
  7.2 0.0 copy-start.6
  7.2 0.0 copy-start.5
  7.2 0.0 copy-start.7
  7.2 0.0 all-gather.5.cloned.1.call-start
  7.3 0.8 reduce-window.8
  8.1 1.3 copy.21
  9.4 0.1 convert_reduce_fusion
  9.5 0.0 copy-done.6
  9.5 0.0 copy-done.5
  9.5 0.1 select_reduce_fusion
  9.6 0.0 copy-done.7
  9.6 5.0 while.15
  9.6 0.1 copy.30
  9.8 0.7 fusion.49
  10.5 0.1 copy.30
  10.6 0.7 fusion.49
  11.3 0.1 copy.30
  11.4 0.7 fusion.49
  12.1 0.1 copy.30
  12.3 0.7 fusion.49
  13.0 0.1 copy.30
  13.1 0.7 fusion.49
  13.8 0.1 copy.30
  13.9 0.7 fusion.49
  14.6 1.6 fusion.13
  16.2 1.7 convolution_bitcast_fusion
  18.0 1.5 fusion.10
  19.5 0.0 copy-start.4
  19.5 0.9 convert_element_type.40
  20.4 0.0 all-gather.5.cloned.1.call-update
  20.4 0.0 all-reduce.4.cloned.1.call-start
  20.4 0.0 copy-done
  20.5 10.5 all-gather
  30.9 0.0 copy-done.4
  31.0 37.2 %all-gather.5.cloned.1.call-done = bf16[1728,512]{1,0:T(8,128)(2,1)} async-done(((bf16[1728,128]{1,0:T(8,128)(2,1)}), bf16[1728,512]{1,0:T(8,128)(2,1)}) %all-gather.5.cloned.1.call-update) | async-done | bytes 1769488 | tf_op jit(solution)/shard_map/all_gather | solution.py:82
  68.2 3.1 fusion.18
  71.3 0.0 all-reduce.4.cloned.1.call-update
  71.3 0.0 all-gather.7.cloned.1.call-start
  71.4 0.1 stack.6
  71.6 0.1 multiply_convert_fusion
  71.7 0.1 convert_element_type.36
  71.8 774.1 %all-reduce.4.cloned.1.call-done = f32[1728,128]{1,0:T(8,128)} async-done(((f32[1728,128]{1,0:T(8,128)}), f32[1728,128]{1,0:T(8,128)}) %all-reduce.4.cloned.1.call-update) | async-done | bytes 884752 | tf_op jit(solution)/shard_map/psum | solution.py:88
  845.9 1.8 convolution_maximum_fusion
  847.7 0.0 copy-start.3
  847.8 0.0 copy-start.8
  847.8 1.5 fusion.41
  849.3 0.0 all-gather.7.cloned.1.call-update
  849.3 0.0 copy-done.8
  849.3 0.6 dynamic-slice.1
  850.5 370.5 %all-gather.7.cloned.1.call-done = f32[110592,128]{1,0:T(8,128)} async-done(((f32[1728,128]{1,0:T(8,128)}), f32[110592,128]{1,0:T(8,128)}) %all-gather.7.cloned.1.call-update) | async-done | bytes 56623120 | tf_op jit(solution)/shard_map/all_gather | solution.py:13
  1221.1 0.0 copy-start.2
  1221.1 0.0 copy-start.1
  1221.1 17.9 %reduce_sum.48 = f32[1728,128]{1,0:T(8,128)S(1)} reduce(f32[64,1728,128]{2,1,0:T(8,128)} %bitcast.31, f32[]{:T(128)} %constant.70.clone.1), dimensions={0}, to_apply=%region_7.8 | reduce | flops 13934592 | bytes 57507844 | tf_op jit(solution)/shard_map/reduce_sum | solution.py:13
  1238.9 0.0 copy-done.3
  1238.9 0.0 copy-done.2
  1238.9 1.1 fusion.15
  1240.0 8.4 all-reduce.1
  1248.4 0.6 dynamic-slice_bitcast_fusion
  1249.0 0.0 copy-done.1
  (18 shorter events, 0.2 us)
Async XLA Ops:
  7.2 13.3 %copy-start = (s32[1,8192]{1,0:T(1,128)S(1)}, s32[1,8192]{1,0:T(1,128)}, u32[]{:S(2)}) copy-start(s32[1,8192]{1,0:T(1,128)} %param.11) | copy-start | bytes 98308
  7.2 2.3 copy-start.6
  7.2 2.3 copy-start.5
  7.2 2.4 copy-start.7
  7.2 61.0 %all-gather.5.cloned.1.call-start = ((), (), s32[]{:S(2)}) async-start(), calls=%async_computation | async-start | bytes 2211840 | tf_op jit(solution)/shard_map/all_gather | solution.py:82
  19.5 11.5 copy-start.4
  20.4 825.5 %all-reduce.4.cloned.1.call-start = ((), (), s32[]{:S(2)}) async-start(), calls=%async_computation.1 | async-start | bytes 1769472 | tf_op jit(solution)/shard_map/psum | solution.py:88
  71.3 1149.7 %all-gather.7.cloned.1.call-start = ((), (), s32[]{:S(2)}) async-start(), calls=%async_computation.2 | async-start | bytes 57507840 | tf_op jit(solution)/shard_map/all_gather | solution.py:13
  847.7 391.2 %copy-start.3 = (f32[128,128]{1,0:T(8,128)}, f32[128,128]{1,0:T(8,128)S(1)}, u32[]{:S(2)}) copy-start(f32[128,128]{1,0:T(8,128)S(1)} %convolution_maximum_fusion) | copy-start | bytes 196612
  847.8 1.5 copy-start.8
  1221.1 17.9 %copy-start.2 = (bf16[1728,512]{1,0:T(8,128)(2,1)S(1)}, bf16[1728,512]{1,0:T(8,128)(2,1)}, u32[]{:S(2)}) copy-start(bf16[1728,512]{1,0:T(8,128)(2,1)} %all-gather.5.cloned.1.call-done) | copy-start | bytes 5308420
  1221.1 27.9 %copy-start.1 = (s32[1,8192]{1,0:T(1,128)S(1)}, s32[1,8192]{1,0:T(1,128)}, u32[]{:S(2)}) copy-start(s32[1,8192]{1,0:T(1,128)} %param.11) | copy-start | bytes 98308
Sparse Core Ops, SparseCore 0:
  20.5 47.6 all-gather.4
  71.4 774.4 all-reduce.3
  849.4 371.5 all-gather.6
